TPU v7x, 256 devices: a whole 4x4x8 slice. The times are simulated.
256 devices in a mesh: fsdp: 16 (over z_hi, x), tensor: 16 (over z_lo, y, core).
Axes of the slice: x: 4, y: 4, z: 8 (z_hi: 4, z_lo: 2; z = z_hi * 2 + z_lo), core: 2. Of those that a mesh axis runs over, the one named last changes fastest.
Arguments:
- tokens: bfloat16 [8192, 3072], P('fsdp'), may hold values from -6 to 6
- weights: bfloat16 [3072, 4, 4096], P('fsdp', None, 'tensor'), may hold values from -0.109375 to 0.109375
- direction: bfloat16 [3072, 4, 4096], P('fsdp', None, 'tensor'), may hold values from -0.109375 to 0.109375
- precision: float32 [3072], replicated, may hold values from 0.25 to 4
Outputs:
- ggn: float32 [3072, 4, 4096], P('fsdp', None, 'tensor')
All inputs are finite; a program needn't handle non-finite values.
Results may differ from a plain program's by a relative error of at most 0.015.
Values may be sent and summed in bfloat16 or wider, within the bound.
No kernel may reach another device: no remote copies, remote signals or barrier semaphores. Data moves between devices by JAX's collectives and lax.ppermute only.
A program may use at most 128 MiB of HBM per device.

v0:
```python
import jax
import jax.numpy as jnp
from jax import lax
from jax.sharding import Mesh, PartitionSpec as P

FSDP = ("z_hi", "x")
TENSOR = ("z_lo", "y", "core")
HEAD = 128
PATCHES = 256


def layer_norm(rows):
    mean_row = jnp.mean(rows, -1, keepdims=True)
    centred = rows - mean_row
    spread = jnp.mean(centred * centred, -1, keepdims=True)
    return centred * lax.rsqrt(spread + 1e-06)


def attend(queries, key_rows, value_rows):
    query_norm = layer_norm(queries)
    key_norm = layer_norm(key_rows)
    score_scale = queries.shape[-1] ** (-0.5)
    scores = (
        jnp.einsum("bqhe,bkhe->bhqk", query_norm, key_norm, precision=lax.Precision.HIGHEST)
        * score_scale
    )
    exponent = jnp.exp(scores)
    attn_weights = exponent / jnp.sum(exponent, -1, keepdims=True)
    return jnp.einsum("bhqk,bkhe->bqhe", attn_weights, value_rows, precision=lax.Precision.HIGHEST)


def cross_rows(left, right):
    return lax.dot_general(
        left, right, (((1,), (1,)), ((), ())), preferred_element_type=jnp.float32
    )


def over_tokens(left, right):
    return lax.dot_general(
        left, right, (((0,), (0,)), ((), ())), preferred_element_type=jnp.float32
    )


def body(tokens, weights, direction, precision):
    model_width = tokens.shape[1]
    local_rows = tokens.shape[0]
    share_rows = weights.shape[0]
    head_cols = weights.shape[2]
    normed = layer_norm(tokens.astype(jnp.float32)).astype(jnp.bfloat16)
    local = jnp.concatenate(
        [weights[:, 0:3], direction[:, 0:3], weights[:, 3:4], direction[:, 3:4]], 1
    ).reshape(share_rows, 8 * head_cols)
    gathered = lax.all_gather(local.T, FSDP, axis=1, tiled=True)
    in_both = gathered[: 6 * head_cols]
    out_both = gathered[6 * head_cols :]
    both_in = cross_rows(normed, in_both).astype(jnp.bfloat16)
    projected = both_in[:, : 3 * head_cols]
    tangent_in = both_in[:, 3 * head_cols :]

    def to_heads(block):
        return block.astype(jnp.float32).reshape(
            local_rows // PATCHES, PATCHES, 3, head_cols // HEAD, HEAD
        )

    primal = to_heads(projected)
    tangent_heads = to_heads(tangent_in)
    primal_args = (primal[:, :, 0], primal[:, :, 1], primal[:, :, 2])
    tangent_args = (tangent_heads[:, :, 0], tangent_heads[:, :, 1], tangent_heads[:, :, 2])
    mixed, mixed_dot = jax.jvp(attend, primal_args, tangent_args)
    mixed_rows = mixed.reshape(local_rows, head_cols).astype(jnp.bfloat16)
    tangent_out = mixed_dot.reshape(local_rows, head_cols).astype(jnp.bfloat16)
    partial_cols = lax.dot_general(
        out_both,
        jnp.concatenate([tangent_out, mixed_rows], 1),
        (((0,), (1,)), ((), ())),
        preferred_element_type=jnp.float32,
    )
    n_tensor = lax.axis_size(TENSOR)
    chunk = model_width // n_tensor
    n_core = lax.axis_size("core")
    n_chip = n_tensor // n_core
    swap = [(0, 1), (1, 0)]
    core_index = lax.axis_index("core")
    by_core = partial_cols.astype(jnp.bfloat16).reshape(n_chip, n_core, chunk, local_rows)
    kept = lax.dynamic_index_in_dim(by_core, core_index, 1, keepdims=False)
    given = lax.dynamic_index_in_dim(by_core, 1 - core_index, 1, keepdims=False)
    received = lax.ppermute(given, "core", swap)
    pair_sum = kept.astype(jnp.float32) + received.astype(jnp.float32)
    arrived = lax.all_to_all(pair_sum.astype(jnp.bfloat16), ("z_lo", "y"), 0, 0)
    output_dot = jnp.sum(arrived.astype(jnp.float32), 0)
    own_precision = lax.dynamic_slice_in_dim(precision, lax.axis_index(TENSOR) * chunk, chunk)
    cotangent_part = (own_precision[:, None] * output_dot).astype(jnp.bfloat16)
    spread = jnp.broadcast_to(cotangent_part[None], (n_chip, chunk, local_rows))
    on_chip = lax.all_to_all(spread, ("z_lo", "y"), 0, 0)
    partner = lax.ppermute(on_chip, "core", swap)
    first = core_index == 0
    cotangent_cols = jnp.stack(
        [jnp.where(first, on_chip, partner), jnp.where(first, partner, on_chip)], 1
    ).reshape(model_width, local_rows)
    back_rows = lax.dot_general(
        cotangent_cols,
        out_both[:head_cols],
        (((0,), (1,)), ((), ())),
        preferred_element_type=jnp.float32,
    )
    back_rows = back_rows.reshape(local_rows // PATCHES, PATCHES, head_cols // HEAD, HEAD)
    primal_out, pullback = jax.vjp(attend, *primal_args)
    gradients = pullback(back_rows)
    stacked = jnp.stack(gradients, axis=2).reshape(local_rows, 3 * head_cols).astype(jnp.bfloat16)
    summed = jnp.concatenate(
        [
            over_tokens(normed, stacked).reshape(model_width, 3, head_cols),
            jnp.dot(cotangent_cols, mixed_rows, preferred_element_type=jnp.float32)[:, None, :],
        ],
        axis=1,
    ).astype(jnp.bfloat16)
    n_hi = lax.axis_size("z_hi")
    n_x = lax.axis_size("x")
    summed = summed.reshape(n_hi, n_x, share_rows, 4, head_cols).swapaxes(0, 1)
    summed = summed.reshape(model_width, 4, head_cols)
    summed = lax.psum_scatter(summed, "x", scatter_dimension=0, tiled=True)
    blocks = summed.reshape(n_hi, share_rows, 4, head_cols)
    hi_index = lax.axis_index("z_hi")
    total = lax.dynamic_index_in_dim(blocks, hi_index, 0, keepdims=False).astype(jnp.float32)
    for shift in sorted(range(1, n_hi), key=lambda k: -min(k, n_hi - k)):
        outgoing = lax.dynamic_index_in_dim(blocks, (hi_index + shift) % n_hi, 0, keepdims=False)
        pairs = [(i, (i + shift) % n_hi) for i in range(n_hi)]
        total = total + lax.ppermute(outgoing, "z_hi", pairs).astype(jnp.float32)
    return total


def solution(mesh):
    n_fsdp, n_tensor = mesh.devices.shape
    n_x = 4 if n_fsdp % 4 == 0 else n_fsdp
    parts = mesh.devices.reshape(n_fsdp // n_x, n_x, 2, n_tensor // 4, 2)
    fine = Mesh(parts, ("z_hi", "x", "z_lo", "y", "core"))
    return jax.shard_map(
        body,
        mesh=fine,
        in_specs=(P(FSDP, None), P(FSDP, None, TENSOR), P(FSDP, None, TENSOR), P()),
        out_specs=P(FSDP, None, TENSOR),
        check_vma=False,
    )
```

profile of v0, /device:TPU:1, one launch (start us, length us, event | category | flops | bytes accessed | tf_op | source)
XLA Modules:
  0.0 423.0 jit_solution(7690654726230957890)
XLA Ops:
  6.5 1.2 slice.48
  7.8 1.2 slice.49
  9.0 2.0 pad_maximum_fusion.1
  12.1 3.2 copy.60
  16.7 2.5 fusion.5
  19.1 146.2 %all-gather.2.cloned.1.call-done = bf16[2048,3072]{0,1:T(8,128)(2,1)} async-done(((bf16[2048,192]{0,1:T(8,128)(2,1)}), bf16[2048,3072]{0,1:T(8,128)(2,1)}) %all-gather.2.cloned.1.call-update) | async-done | bytes 12582928 | tf_op jit(solution)/shard_map/all_gather | solution.py:53
  165.3 9.4 %fusion.10 = bf16[512,1536]{1,0:T(8,128)(2,1)S(1)} fusion(bf16[512,3072]{0,1:T(8,128)(2,1)} %fusion.5, bf16[2048,3072]{0,1:T(8,128)(2,1)} %all-gather.2.cloned.1.call-done), kind=kOutput, calls=%fused_computation.17 | convolution fusion | flops 4832624640 | bytes 14155776 | tf_op jit(solution)/shard_map/dot_general | solution.py:33
  176.3 1.2 copy.62
  178.3 1.2 fusion.76
  179.5 1.5 fusion.55
  181.0 1.3 fusion.23
  182.3 1.1 fusion.40
  183.4 1.3 fusion.77
  184.7 1.4 fusion.25
  186.1 1.8 copy.73
  187.9 1.7 copy.127
  189.6 1.8 copy.75
  192.5 3.7 convolution_convert_fusion
  196.2 1.4 dynamic-slice_bitcast_fusion
  199.2 3.4 collective-permute-done
  202.6 3.5 fusion.7
  206.1 14.4 %all-to-all-start = ((bf16[8,192,512]{2,1,0:T(8,128)(2,1)}), bf16[8,192,512]{2,1,0:T(8,128)(2,1)}, u32[]{:S(2)}, u32[]{:S(2)}) async-start(bf16[8,192,512]{2,1,0:T(8,128)(2,1)} %fusion.7), calls=%async_computation | async-start | bytes 3145728 | tf_op jit(solution)/shard_map/all_to_all | solution.py:89
  221.4 19.9 %all-to-all-done = bf16[8,192,512]{2,1,0:T(8,128)(2,1)} async-done(((bf16[8,192,512]{2,1,0:T(8,128)(2,1)}), bf16[8,192,512]{2,1,0:T(8,128)(2,1)}, u32[]{:S(2)}, u32[]{:S(2)}) %all-to-all-start) | async-done | bytes 1572896 | tf_op jit(solution)/shard_map/all_to_all | solution.py:89
  241.2 1.7 convert_reduce_fusion.1
  243.1 23.6 %all_to_all.10 = bf16[8,192,512]{2,1,0:T(8,128)(2,1)} all-to-all(bf16[8,192,512]{2,1,0:T(8,128)(2,1)S(1)} %broadcast_in_dim.12), channel_id=1, replica_groups=mesh['z_hi'=4,'x'=4,'z_lo'=2,'y'=4,'core'=2] {'z_lo','y'}, dimensions={0} | all-to-all | bytes 3145728 | tf_op jit(solution)/shard_map/all_to_all | solution.py:94
  266.7 2.4 collective-permute-start.1
  269.1 1.8 reshape.188
  270.9 2.7 slice.71
  273.6 2.6 copy.78
  276.2 2.1 select_bitcast_fusion.1
  278.3 2.0 pad_maximum_fusion
  280.2 4.7 %copy.77 = bf16[512,3072]{1,0:T(8,128)(2,1)} copy(bf16[512,3072]{0,1:T(8,128)(2,1)} %bitcast.195) | data formatting | bytes 6291456 | tf_op jit(solution)/shard_map/dot_general | solution.py:100
  284.9 3.4 convolution_bitcast_fusion.2
  288.3 1.3 fusion.24
  291.3 1.5 fusion.70
  293.4 1.8 copy.85
  295.2 3.3 convert_element_type.93
  298.4 2.3 copy.86
  302.8 3.1 convolution_convert_fusion.1
  306.5 3.1 copy.87
  309.6 61.7 %reduce-scatter.2.cloned.1.call-done = bf16[768,4,256]{2,0,1:T(8,128)(2,1)} async-done(((bf16[3072,4,256]{2,0,1:T(8,128)(2,1)}), bf16[768,4,256]{2,0,1:T(8,128)(2,1)}) %reduce-scatter.2.cloned.1.call-update) | async-done | bytes 1572880 | tf_op jit(solution)/shard_map/reduce_scatter | solution.py:121
  371.3 1.5 constant_dynamic-slice_fusion.3
  373.8 5.5 %collective-permute-start.2 = (bf16[192,4,256]{2,1,0:T(4,128)(2,1)S(1)}, bf16[192,4,256]{2,1,0:T(4,128)(2,1)S(1)}, u32[]{:S(2)}, u32[]{:S(2)}) collective-permute-start(bf16[192,4,256]{2,1,0:T(4,128)(2,1)S(1)} %bitcast.214), channel_id=1, source_target_pairs={{0,128},{64,192},{128,0},{192,64},{1,129},{65,193},{129,1},{193,65... | collective-permute-start | bytes 1179656 | tf_op jit(solution)/shard_map/ppermute | solution.py:128
  379.8 3.1 collective-permute-start.4
  382.9 8.8 %collective-permute-done.2 = bf16[192,4,256]{2,1,0:T(4,128)(2,1)S(1)} collective-permute-done((bf16[192,4,256]{2,1,0:T(4,128)(2,1)S(1)}, bf16[192,4,256]{2,1,0:T(4,128)(2,1)S(1)}, u32[]{:S(2)}, u32[]{:S(2)}) %collective-permute-start.2) | collective-permute-done | bytes 393248 | tf_op jit(solution)/shard_map/ppermute | solution.py:128
  391.7 16.6 %collective-permute-done.3 = bf16[192,4,256]{2,1,0:T(4,128)(2,1)S(1)} collective-permute-done((bf16[192,4,256]{2,1,0:T(4,128)(2,1)S(1)}, bf16[192,4,256]{2,1,0:T(4,128)(2,1)S(1)}, u32[]{:S(2)}, u32[]{:S(2)}) %collective-permute-start.3) | collective-permute-done | bytes 393248 | tf_op jit(solution)/shard_map/ppermute | solution.py:128
  408.3 6.4 %collective-permute-done.4 = bf16[192,4,256]{2,1,0:T(4,128)(2,1)S(1)} collective-permute-done((bf16[192,4,256]{2,1,0:T(4,128)(2,1)S(1)}, bf16[192,4,256]{2,1,0:T(4,128)(2,1)S(1)}, u32[]{:S(2)}, u32[]{:S(2)}) %collective-permute-start.4) | collective-permute-done | bytes 393248 | tf_op jit(solution)/shard_map/ppermute | solution.py:128
  414.8 1.4 fusion.31
  (58 shorter events, 14.6 us)
Async XLA Ops:
  6.5 158.8 %all-gather.2.cloned.1.call-start = ((), (), s32[]{:S(2)}) async-start(), calls=%async_computation.3 | async-start | bytes 13369344 | tf_op jit(solution)/shard_map/all_gather | solution.py:53
  176.1 1.7 copy-start.2
  196.2 2.2 copy-start.1
  198.4 4.2 collective-permute-start
  206.1 35.1 %all-to-all-start = ((bf16[8,192,512]{2,1,0:T(8,128)(2,1)}), bf16[8,192,512]{2,1,0:T(8,128)(2,1)}, u32[]{:S(2)}, u32[]{:S(2)}) async-start(bf16[8,192,512]{2,1,0:T(8,128)(2,1)} %fusion.7), calls=%async_computation | async-start | bytes 3145728 | tf_op jit(solution)/shard_map/all_to_all | solution.py:89
  220.5 150.8 %reduce-scatter.2.cloned.1.call-start = ((), (), s32[]{:S(2)}) async-start(), calls=%async_computation.4 | async-start | bytes 7864320 | tf_op jit(solution)/shard_map/reduce_scatter | solution.py:121
  266.7 9.5 %collective-permute-start.1 = (bf16[8,192,512]{2,1,0:T(8,128)(2,1)}, bf16[8,192,512]{2,1,0:T(8,128)(2,1)}, u32[]{:S(2)}, u32[]{:S(2)}) collective-permute-start(bf16[8,192,512]{2,1,0:T(8,128)(2,1)} %all_to_all.10), channel_id=1, source_target_pairs={{0,1},{1,0},{2,3},{3,2},{4,5},{5,4},{6,7},{7,6},{8,9},{9,8},{10,11... | collective-permute-start | bytes 4718600 | tf_op jit(solution)/shard_map/ppermute | solution.py:95
  293.3 7.4 %copy-start.4 = (bf16[512,256,1,1]{1,0,2,3:T(8,128)(2,1)S(1)}, bf16[512,256,1,1]{1,0,2,3:T(8,128)(2,1)}, u32[]{:S(2)}) copy-start(bf16[512,256,1,1]{1,0,2,3:T(8,128)(2,1)} %reshape.188) | copy-start | bytes 786436
  295.2 5.6 %copy-start = (bf16[8,2,192,512]{3,2,1,0:T(8,128)(2,1)S(1)}, bf16[8,2,192,512]{3,2,1,0:T(8,128)(2,1)}, u32[]{:S(2)}) copy-start(bf16[8,2,192,512]{3,2,1,0:T(8,128)(2,1)} %pad_maximum_fusion) | copy-start | bytes 9437188
  300.7 1.9 copy-start.3
  300.7 2.1 copy-start.5
  373.8 18.0 %collective-permute-start.2 = (bf16[192,4,256]{2,1,0:T(4,128)(2,1)S(1)}, bf16[192,4,256]{2,1,0:T(4,128)(2,1)S(1)}, u32[]{:S(2)}, u32[]{:S(2)}) collective-permute-start(bf16[192,4,256]{2,1,0:T(4,128)(2,1)S(1)} %bitcast.214), channel_id=1, source_target_pairs={{0,128},{64,192},{128,0},{192,64},{1,129},{65,193},{129,1},{193,65... | collective-permute-start | bytes 1179656 | tf_op jit(solution)/shard_map/ppermute | solution.py:128
  379.3 29.0 %collective-permute-start.3 = (bf16[192,4,256]{2,1,0:T(4,128)(2,1)S(1)}, bf16[192,4,256]{2,1,0:T(4,128)(2,1)S(1)}, u32[]{:S(2)}, u32[]{:S(2)}) collective-permute-start(bf16[192,4,256]{2,1,0:T(4,128)(2,1)S(1)} %bitcast.213), channel_id=1, source_target_pairs={{0,64},{64,128},{128,192},{192,0},{1,65},{65,129},{129,193},{193,1... | collective-permute-start | bytes 1179656 | tf_op jit(solution)/shard_map/ppermute | solution.py:128
  379.8 35.0 %collective-permute-start.4 = (bf16[192,4,256]{2,1,0:T(4,128)(2,1)S(1)}, bf16[192,4,256]{2,1,0:T(4,128)(2,1)S(1)}, u32[]{:S(2)}, u32[]{:S(2)}) collective-permute-start(bf16[192,4,256]{2,1,0:T(4,128)(2,1)S(1)} %bitcast.212), channel_id=1, source_target_pairs={{0,192},{64,0},{128,64},{192,128},{1,193},{65,1},{129,65},{193,129... | collective-permute-start | bytes 1179656 | tf_op jit(solution)/shard_map/ppermute | solution.py:128
Sparse Core Ops, SparseCore 0:
  12.2 153.0 all-gather.1
  309.7 61.5 reduce-scatter.1
where the time goes:
time: 424 us; the launch traced here: 423 us
  waiting for transfers between devices  263 us (62%)
  local copies, waits for them, and re-layouts  44.5 us (10%)
  matrix products  32.8 us (8%)
  starting transfers between devices  26.8 us (6%)
  blocking collectives  23.6 us (6%)
  other arithmetic  18.5 us (4%)
  between operations  13.8 us (3%)
    all_gather x1, waiting for transfers between devices, body(): gathered = lax.all_gather(local.T, FSDP, axis=1, tiled=True)  146 us
    reduce_scatter x1, waiting for transfers between devices, body(): summed = lax.psum_scatter(summed, 'x', scatter_dimension=0, tiled=True)  61.7 us
    ppermute x3, waiting for transfers between devices, body(): total = total + lax.ppermute(outgoing, 'z_hi', pairs).astype(jnp.float32)  31.9 us
    all_to_all x1, blocking collectives, body(): on_chip = lax.all_to_all(spread, ('z_lo', 'y'), 0, 0)  23.6 us
    all_to_all x1, waiting for transfers between devices, body(): arrived = lax.all_to_all(pair_sum.astype(jnp.bfloat16), ('z_lo', 'y'), 0, 0)  19.9 us
    all_to_all x1, starting transfers between devices, body(): arrived = lax.all_to_all(pair_sum.astype(jnp.bfloat16), ('z_lo', 'y'), 0, 0)  14.4 us
    dot_general x1, matrix products, cross_rows(): lax.dot_general(left, right, (((1,), (1,)), ((), ())), preferred_element_...  9.42 us
    ppermute x3, starting transfers between devices, body(): total = total + lax.ppermute(outgoing, 'z_hi', pairs).astype(jnp.float32)  9.12 us
  transfers between devices with their start and end apart: 8, of which 7 were waited for; matrix products, arithmetic and copies ran while one was open for 4% of the time, Pallas kernels for 0%

commit v1 on v0

--- a/solution.py
+++ b/solution.py
@@ -42,6 +42,18 @@
 
 
 def body(tokens, weights, direction, precision):
+
+    def view_open(arr):
+        return jnp.concatenate(
+            lax.all_to_all(
+                jnp.stack([arr] * lax.axis_size(FSDP), axis=0),
+                axis_name=FSDP,
+                split_axis=0,
+                concat_axis=0,
+            ),
+            1,
+        )
+
     model_width = tokens.shape[1]
     local_rows = tokens.shape[0]
     share_rows = weights.shape[0]
@@ -50,7 +62,7 @@
     local = jnp.concatenate(
         [weights[:, 0:3], direction[:, 0:3], weights[:, 3:4], direction[:, 3:4]], 1
     ).reshape(share_rows, 8 * head_cols)
-    gathered = lax.all_gather(local.T, FSDP, axis=1, tiled=True)
+    gathered = view_open(local.T)
     in_both = gathered[: 6 * head_cols]
     out_both = gathered[6 * head_cols :]
     both_in = cross_rows(normed, in_both).astype(jnp.bfloat16)

time: 424 us -> 592 us (1.40); the launches traced: 423 us -> 584 us
  waiting for transfers between devices: 263 us -> 379 us
  starting transfers between devices: 26.8 us -> 48.9 us
  local copies, waits for them, and re-layouts: 44.5 us -> 65.5 us
    all_to_all x0 -> x1, waiting for transfers between devices: none -> 258 us  [view_open(): lax.all_to_all(jnp.stack([arr] * lax.axis_size(FSDP), axis=0), axis_name=...]
    all_gather x1 -> x0, waiting for transfers between devices: 146 us -> none  [body(): gathered = lax.all_gather(local.T, FSDP, axis=1, tiled=True)]
    slice x0 -> x2, local copies, waits for them, and re-layouts: none -> 12.1 us  [the longest x1 8.23 us: body(): in_both = gathered[:6 * head_cols]]
    all_to_all x0 -> x1, starting transfers between devices: none -> 11.6 us  [view_open(): lax.all_to_all(jnp.stack([arr] * lax.axis_size(FSDP), axis=0), axis_name=...]
    all_to_all x1, starting transfers between devices: 14.4 us -> 23.6 us  [body(): arrived = lax.all_to_all(pair_sum.astype(jnp.bfloat16), ('z_lo', 'y'), 0, 0)]
    dot_general x1 -> x3, local copies, waits for them, and re-layouts: 4.69 us -> 13.4 us  [body(): lax.dot_general(cotangent_cols, out_both[:head_cols], (((0,), (1,)), ((),...]
    another operation x0 -> x1, local copies, waits for them, and re-layouts: none -> 6.08 us  [view_open(): jnp.stack([arr] * lax.axis_size(FSDP), axis=0)]
where the time goes in v1:
time: 592 us; the launch traced here: 584 us
  waiting for transfers between devices  379 us (64%)
  local copies, waits for them, and re-layouts  65.5 us (11%)
  starting transfers between devices  48.9 us (8%)
  matrix products  32.8 us (6%)
  blocking collectives  23.6 us (4%)
  other arithmetic  19.7 us (3%)
  between operations  14.1 us (2%)
    all_to_all x1, waiting for transfers between devices, view_open(): lax.all_to_all(jnp.stack([arr] * lax.axis_size(FSDP), axis=0), axis_name=...  258 us
    reduce_scatter x1, waiting for transfers between devices, body(): summed = lax.psum_scatter(summed, 'x', scatter_dimension=0, tiled=True)  67 us
    ppermute x3, waiting for transfers between devices, body(): total = total + lax.ppermute(outgoing, 'z_hi', pairs).astype(jnp.float32)  31.1 us
    all_to_all x1, blocking collectives, body(): on_chip = lax.all_to_all(spread, ('z_lo', 'y'), 0, 0)  23.6 us
    all_to_all x1, starting transfers between devices, body(): arrived = lax.all_to_all(pair_sum.astype(jnp.bfloat16), ('z_lo', 'y'), 0, 0)  23.6 us
    all_to_all x1, waiting for transfers between devices, body(): arrived = lax.all_to_all(pair_sum.astype(jnp.bfloat16), ('z_lo', 'y'), 0, 0)  19.9 us
    dot_general x3, local copies, waits for them, and re-layouts, body(): lax.dot_general(cotangent_cols, out_both[:head_cols], (((0,), (1,)), ((),...  13.4 us
  transfers between devices with their start and end apart: 8, of which 7 were waited for; matrix products, arithmetic and copies ran while one was open for 4% of the time, Pallas kernels for 0%

profile of v1, /device:TPU:1, one launch (start us, length us, event | category | flops | bytes accessed | tf_op | source)
XLA Modules:
  0.0 584.0 jit_solution(16282878200279378111)
XLA Ops:
  9.0 2.0 pad_maximum_fusion.1
  11.2 6.1 %stack.20 = bf16[16,2048,192]{1,2,0:T(8,128)(2,1)} broadcast(bf16[2048,192]{0,1:T(8,128)(2,1)S(1)} %bitcast.207), dimensions={1,2} | broadcast | bytes 13369344 | tf_op jit(solution)/shard_map/stack | solution.py:49
  17.3 11.6 %all-to-all-start = ((bf16[16,2048,192]{1,2,0:T(8,128)(2,1)}), bf16[16,2048,192]{1,2,0:T(8,128)(2,1)}, u32[]{:S(2)}, u32[]{:S(2)}) async-start(bf16[16,2048,192]{1,2,0:T(8,128)(2,1)} %stack.20), calls=%async_computation | async-start | bytes 25165824 | tf_op jit(solution)/shard_map/all_to_all | solution.py:48
  28.9 3.2 copy.28
  33.5 2.5 fusion.3
  36.0 258.1 %all-to-all-done = bf16[16,2048,192]{1,2,0:T(8,128)(2,1)} async-done(((bf16[16,2048,192]{1,2,0:T(8,128)(2,1)}), bf16[16,2048,192]{1,2,0:T(8,128)(2,1)}, u32[]{:S(2)}, u32[]{:S(2)}) %all-to-all-start) | async-done | bytes 12582944 | tf_op jit(solution)/shard_map/all_to_all | solution.py:48
  294.1 8.2 %slice.71 = bf16[1536,16,192]{0,2,1:T(8,128)(2,1)} slice(bf16[2048,16,192]{0,2,1:T(8,128)(2,1)} %bitcast.5), slice={[0:1536], [0:16], [0:192]} | slice | bytes 18874368 | tf_op jit(solution)/shard_map/slice | solution.py:66
  302.4 7.8 %convolution_convert_fusion.1 = bf16[512,1536]{1,0:T(8,128)(2,1)S(1)} fusion(bf16[512,3072]{0,1:T(8,128)(2,1)S(1)} %copy-done.2, bf16[1536,3072]{0,1:T(8,128)(2,1)} %bitcast.206), kind=kOutput, calls=%fused_computation.14 | convolution fusion | flops 4832624640 | bytes 14155776 | tf_op jit(solution)/shard_map/dot_general | solution.py:33
  312.6 2.0 reshape.185
  314.7 2.5 copy.29
  317.2 1.3 reshape.188
  320.1 1.5 fusion.54
  322.9 3.8 slice.70
  329.2 1.4 fusion.24
  330.6 1.8 copy.41
  332.4 1.7 copy.95
  334.1 1.8 copy.43
  336.9 3.7 convolution_convert_fusion
  340.6 1.4 dynamic-slice_bitcast_fusion
  342.9 2.0 collective-permute-start
  344.8 3.4 collective-permute-done
  348.2 3.6 fusion.4
  351.8 23.6 %all-to-all-start.1 = ((bf16[8,192,512]{2,1,0:T(8,128)(2,1)}), bf16[8,192,512]{2,1,0:T(8,128)(2,1)}, u32[]{:S(2)}, u32[]{:S(2)}) async-start(bf16[8,192,512]{2,1,0:T(8,128)(2,1)} %fusion.4), calls=%async_computation.1 | async-start | bytes 3145728 | tf_op jit(solution)/shard_map/all_to_all | solution.py:101
  376.2 19.9 %all-to-all-done.1 = bf16[8,192,512]{2,1,0:T(8,128)(2,1)} async-done(((bf16[8,192,512]{2,1,0:T(8,128)(2,1)}), bf16[8,192,512]{2,1,0:T(8,128)(2,1)}, u32[]{:S(2)}, u32[]{:S(2)}) %all-to-all-start.1) | async-done | bytes 1572896 | tf_op jit(solution)/shard_map/all_to_all | solution.py:101
  396.0 1.7 convert_reduce_fusion.1
  397.9 23.6 %all_to_all.15 = bf16[8,192,512]{2,1,0:T(8,128)(2,1)} all-to-all(bf16[8,192,512]{2,1,0:T(8,128)(2,1)S(1)} %broadcast_in_dim.12), channel_id=1, replica_groups=mesh['z_hi'=4,'x'=4,'z_lo'=2,'y'=4,'core'=2] {'z_lo','y'}, dimensions={0} | all-to-all | bytes 3145728 | tf_op jit(solution)/shard_map/all_to_all | solution.py:106
  421.5 2.4 collective-permute-start.1
  423.9 2.7 slice.80
  426.6 1.8 reshape.199
  428.4 3.7 dot_general.76
  432.2 5.0 copy.46
  437.1 2.1 select_bitcast_fusion.1
  439.2 2.0 pad_maximum_fusion
  441.2 4.7 copy.45
  445.9 3.4 fusion.18
  449.9 1.3 fusion.23
  452.3 1.5 fusion.69
  454.3 1.3 copy.53
  456.3 4.7 convolution_convert_fusion.2
  462.6 3.1 copy.55
  465.7 67.0 %reduce-scatter.2.cloned.1.call-done = bf16[768,4,256]{2,0,1:T(8,128)(2,1)} async-done(((bf16[3072,4,256]{2,0,1:T(8,128)(2,1)}), bf16[768,4,256]{2,0,1:T(8,128)(2,1)}) %reduce-scatter.2.cloned.1.call-update) | async-done | bytes 1572880 | tf_op jit(solution)/shard_map/reduce_scatter | solution.py:133
  532.6 1.5 constant_dynamic-slice_fusion.3
  534.5 5.5 collective-permute-start.2
  541.2 3.2 collective-permute-start.4
  544.3 7.9 %collective-permute-done.2 = bf16[192,4,256]{2,1,0:T(4,128)(2,1)S(1)} collective-permute-done((bf16[192,4,256]{2,1,0:T(4,128)(2,1)S(1)}, bf16[192,4,256]{2,1,0:T(4,128)(2,1)S(1)}, u32[]{:S(2)}, u32[]{:S(2)}) %collective-permute-start.2) | collective-permute-done | bytes 393248 | tf_op jit(solution)/shard_map/ppermute | solution.py:140
  552.2 14.3 %collective-permute-done.3 = bf16[192,4,256]{2,1,0:T(4,128)(2,1)S(1)} collective-permute-done((bf16[192,4,256]{2,1,0:T(4,128)(2,1)S(1)}, bf16[192,4,256]{2,1,0:T(4,128)(2,1)S(1)}, u32[]{:S(2)}, u32[]{:S(2)}) %collective-permute-start.3) | collective-permute-done | bytes 393248 | tf_op jit(solution)/shard_map/ppermute | solution.py:140
  566.5 8.9 %collective-permute-done.4 = bf16[192,4,256]{2,1,0:T(4,128)(2,1)S(1)} collective-permute-done((bf16[192,4,256]{2,1,0:T(4,128)(2,1)S(1)}, bf16[192,4,256]{2,1,0:T(4,128)(2,1)S(1)}, u32[]{:S(2)}, u32[]{:S(2)}) %collective-permute-start.4) | collective-permute-done | bytes 393248 | tf_op jit(solution)/shard_map/ppermute | solution.py:140
  575.4 1.4 fusion.30
  (57 shorter events, 20.4 us)
Async XLA Ops:
  17.3 276.9 %all-to-all-start = ((bf16[16,2048,192]{1,2,0:T(8,128)(2,1)}), bf16[16,2048,192]{1,2,0:T(8,128)(2,1)}, u32[]{:S(2)}, u32[]{:S(2)}) async-start(bf16[16,2048,192]{1,2,0:T(8,128)(2,1)} %stack.20), calls=%async_computation | async-start | bytes 25165824 | tf_op jit(solution)/shard_map/all_to_all | solution.py:48
  294.1 8.2 %copy-start.2 = (bf16[512,3072]{0,1:T(8,128)(2,1)S(1)}, bf16[512,3072]{0,1:T(8,128)(2,1)}, u32[]{:S(2)}) copy-start(bf16[512,3072]{0,1:T(8,128)(2,1)} %fusion.3) | copy-start | bytes 9437188
  340.6 2.2 copy-start.1
  342.9 5.4 collective-permute-start
  351.8 44.2 %all-to-all-start.1 = ((bf16[8,192,512]{2,1,0:T(8,128)(2,1)}), bf16[8,192,512]{2,1,0:T(8,128)(2,1)}, u32[]{:S(2)}, u32[]{:S(2)}) async-start(bf16[8,192,512]{2,1,0:T(8,128)(2,1)} %fusion.4), calls=%async_computation.1 | async-start | bytes 3145728 | tf_op jit(solution)/shard_map/all_to_all | solution.py:101
  375.3 157.3 %reduce-scatter.2.cloned.1.call-start = ((), (), s32[]{:S(2)}) async-start(), calls=%async_computation.4 | async-start | bytes 7864320 | tf_op jit(solution)/shard_map/reduce_scatter | solution.py:133
  421.5 15.6 %collective-permute-start.1 = (bf16[8,192,512]{2,1,0:T(8,128)(2,1)}, bf16[8,192,512]{2,1,0:T(8,128)(2,1)}, u32[]{:S(2)}, u32[]{:S(2)}) collective-permute-start(bf16[8,192,512]{2,1,0:T(8,128)(2,1)} %all_to_all.15), channel_id=1, source_target_pairs={{0,1},{1,0},{2,3},{3,2},{4,5},{5,4},{6,7},{7,6},{8,9},{9,8},{10,11... | collective-permute-start | bytes 4718600 | tf_op jit(solution)/shard_map/ppermute | solution.py:107
  456.3 4.7 copy-start
  456.3 4.7 copy-start.3
  534.5 17.8 %collective-permute-start.2 = (bf16[192,4,256]{2,1,0:T(4,128)(2,1)S(1)}, bf16[192,4,256]{2,1,0:T(4,128)(2,1)S(1)}, u32[]{:S(2)}, u32[]{:S(2)}) collective-permute-start(bf16[192,4,256]{2,1,0:T(4,128)(2,1)S(1)} %bitcast.221), channel_id=1, source_target_pairs={{0,128},{64,192},{128,0},{192,64},{1,129},{65,193},{129,1},{193,65... | collective-permute-start | bytes 1179656 | tf_op jit(solution)/shard_map/ppermute | solution.py:140
  540.3 26.2 %collective-permute-start.3 = (bf16[192,4,256]{2,1,0:T(4,128)(2,1)S(1)}, bf16[192,4,256]{2,1,0:T(4,128)(2,1)S(1)}, u32[]{:S(2)}, u32[]{:S(2)}) collective-permute-start(bf16[192,4,256]{2,1,0:T(4,128)(2,1)S(1)} %bitcast.222), channel_id=1, source_target_pairs={{0,64},{64,128},{128,192},{192,0},{1,65},{65,129},{129,193},{193,1... | collective-permute-start | bytes 1179656 | tf_op jit(solution)/shard_map/ppermute | solution.py:140
  541.2 34.3 %collective-permute-start.4 = (bf16[192,4,256]{2,1,0:T(4,128)(2,1)S(1)}, bf16[192,4,256]{2,1,0:T(4,128)(2,1)S(1)}, u32[]{:S(2)}, u32[]{:S(2)}) collective-permute-start(bf16[192,4,256]{2,1,0:T(4,128)(2,1)S(1)} %bitcast.223), channel_id=1, source_target_pairs={{0,192},{64,0},{128,64},{192,128},{1,193},{65,1},{129,65},{193,129... | collective-permute-start | bytes 1179656 | tf_op jit(solution)/shard_map/ppermute | solution.py:140
Sparse Core Ops, SparseCore 0:
  465.8 66.8 reduce-scatter.1
